TPU v7x, 512 devices: a whole 4x4x16 slice. The times are simulated.
512 devices in a mesh: ctx: 32 (over x, y, core), head: 16 (over z).
Axes of the slice: x: 4, y: 4, z: 16, core: 2. Of those that a mesh axis runs over, the one named last changes fastest.
Arguments:
- q_linear: bfloat16 [8192, 8192], P('ctx', 'head'), may hold values from -4 to 4
- k_linear: bfloat16 [8192, 8192], P('ctx', 'head'), may hold values from -4 to 4
- v_linear: bfloat16 [8192, 8192], P('ctx', 'head'), may hold values from -40 to 40
- log_decay: float32 [8192, 64], P('ctx', 'head'), may hold values from -1 to 0
- norm_gain: float32 [8192], P('head'), may hold values from 0.5 to 1.5
- q_soft: bfloat16 [8192, 8192], P('ctx', 'head'), may hold values from -6 to 6
- k_soft: bfloat16 [8192, 1024], P('ctx'), may hold values from -4 to 4
- v_soft: bfloat16 [8192, 1024], P('ctx'), may hold values from -4 to 4
Outputs:
- linear_out: bfloat16 [8192, 8192], P('ctx', 'head')
- soft_out: bfloat16 [8192, 8192], P('ctx', 'head')
All inputs are finite; a program needn't handle non-finite values.
Results may differ from a plain program's by a relative error of at most 0.0075.
Values may be sent and summed in bfloat16 or wider, within the bound.
No kernel may reach another device: no remote copies, remote signals or barrier semaphores. Data moves between devices by JAX's collectives and lax.ppermute only.
A program may use at most 64 MiB of HBM per device.

v0:
```python
import jax
import jax.numpy as jnp
from jax import lax
from jax.sharding import PartitionSpec as P

QUERY_HEADS = 64
DH = 128
KV_HEADS = 8
BLOCK = 256
EPSILON = 1e-06
NEGATIVE = -1e30


def shifted(value, axis, steps):
    count = lax.axis_size(axis)
    first, last = (max(0, -steps), min(count, count - steps))
    return lax.ppermute(value, axis, [(source, source + steps) for source in range(first, last)])


def lightning_step(carry, inputs):
    running, log_before = carry
    queries, key_rows, value_rows, log_gates = inputs
    row_count = queries.shape[0]
    cumulative = jnp.cumsum(log_gates, axis=0)
    final_log = cumulative[-1]
    positions = jnp.arange(row_count, dtype=jnp.int32)
    causal = positions[None, :] <= positions[:, None]
    cum_heads = cumulative.T
    log_gap = jnp.where(causal[None], cum_heads[:, :, None] - cum_heads[:, None, :], NEGATIVE)
    scores = jnp.einsum("thd,shd->hts", queries, key_rows, preferred_element_type=jnp.float32)
    weights = (scores * jnp.exp(log_gap)).astype(jnp.bfloat16)
    intra_part = jnp.einsum("hts,she->the", weights, value_rows, preferred_element_type=jnp.float32)
    query_wide = queries.astype(jnp.float32)
    lifted_here = query_wide * jnp.exp(cumulative)[:, :, None]
    carried_here = jnp.einsum("thd,hde->the", lifted_here, running, precision=lax.Precision.HIGHEST)
    lifted_device = query_wide * jnp.exp(cumulative + log_before[None, :])[:, :, None]
    scaled = (key_rows * jnp.exp(final_log[None, :] - cumulative)[:, :, None]).astype(jnp.bfloat16)
    block_state = jnp.einsum("shd,she->hde", scaled, value_rows, preferred_element_type=jnp.float32)
    running = jnp.exp(final_log)[:, None, None] * running + block_state
    return ((running, log_before + final_log), (intra_part + carried_here, lifted_device))


def soft_update(running, queries, query_pos, key_rows, value_rows, key_pos):
    row_max, row_total, weighted = running
    head_count, row_count = row_max.shape
    kv_count, group_local = (queries.shape[1], queries.shape[2])
    scores = jnp.einsum("tkgd,skd->kgts", queries, key_rows, preferred_element_type=jnp.float32)
    scores = scores.reshape(head_count, row_count, key_rows.shape[0]) * DH ** (-0.5)
    allowed = key_pos[None, :] <= query_pos[:, None]
    scores = jnp.where(allowed[None], scores, NEGATIVE)
    new_max = jnp.maximum(row_max, jnp.max(scores, axis=2))
    probabilities = jnp.where(allowed[None], jnp.exp(scores - new_max[:, :, None]), 0.0)
    rescale = jnp.exp(row_max - new_max)
    row_total = row_total * rescale + jnp.sum(probabilities, axis=2)
    rounded = probabilities.astype(jnp.bfloat16).reshape(
        kv_count, group_local, row_count, key_rows.shape[0]
    )
    product = jnp.einsum(
        "kgts,ske->kgte", rounded, value_rows, preferred_element_type=jnp.float32
    ).reshape(head_count, row_count, DH)
    weighted = weighted * rescale[:, :, None] + product
    return (new_max, row_total, weighted)


def over_blocks(running, pieces, row_count, visitor):
    key_rows, value_rows = pieces

    def one_block(block_index, inner_state):
        block_start = block_index * row_count
        keys_here = lax.dynamic_slice_in_dim(key_rows, block_start, row_count, 0)
        values_here = lax.dynamic_slice_in_dim(value_rows, block_start, row_count, 0)
        return visitor(inner_state, keys_here, values_here, block_start)

    return lax.fori_loop(0, key_rows.shape[0] // row_count, one_block, running)


def finish(row_total, weighted, row_count, width):
    return (
        jnp.transpose(weighted / row_total[:, :, None], (1, 0, 2))
        .reshape(row_count, width)
        .astype(jnp.bfloat16)
    )


def local(q_linear, k_linear, v_linear, log_decay, norm_gain, q_soft, k_soft, v_soft):
    row_count = q_linear.shape[0]
    head_count = log_decay.shape[1]
    width = head_count * DH
    local_blocks = row_count // BLOCK
    lin_shape = (local_blocks, BLOCK, head_count, DH)
    sequences = (
        q_linear.reshape(lin_shape),
        k_linear.reshape(lin_shape),
        v_linear.reshape(lin_shape),
        log_decay.reshape(local_blocks, BLOCK, head_count),
    )
    start_carry = (
        jnp.zeros((head_count, DH, DH), jnp.float32),
        jnp.zeros((head_count,), jnp.float32),
    )
    (block_state, log_total), (local_part, lifted) = lax.scan(
        lightning_step, start_carry, sequences
    )
    local_part = local_part.reshape(row_count, head_count, DH)
    lifted = lifted.reshape(row_count, head_count, DH)
    block_fade = jnp.exp(log_total)

    def advance(step_index, entering):
        leaving = block_fade[:, None, None] * entering + block_state
        return shifted(leaving, "ctx", 1)

    entering = lax.fori_loop(0, lax.axis_size("ctx") - 1, advance, jnp.zeros_like(block_state))
    carried = jnp.einsum("thd,hde->the", lifted, entering, precision=lax.Precision.HIGHEST)
    mixed = (local_part + carried).reshape(row_count, width)
    power = lax.psum(jnp.sum(mixed * mixed, axis=1), "head") / (QUERY_HEADS * DH)
    linear_out = (mixed * lax.rsqrt(power + EPSILON)[:, None] * norm_gain[None, :]).astype(
        jnp.bfloat16
    )
    group_size = QUERY_HEADS // KV_HEADS
    kv_count = max(1, head_count // group_size)
    group_local = head_count // kv_count
    kv_start = lax.axis_index("head") * head_count // group_size
    k_local = lax.dynamic_slice_in_dim(k_soft, kv_start * DH, kv_count * DH, 1)
    v_local = lax.dynamic_slice_in_dim(v_soft, kv_start * DH, kv_count * DH, 1)
    query_shape = (row_count, kv_count, group_local, DH)
    key_shape = (row_count, kv_count, DH)
    my_index = lax.axis_index("ctx")
    positions = jnp.arange(row_count, dtype=jnp.int32)
    initial = (
        jnp.full((head_count, row_count), NEGATIVE, jnp.float32),
        jnp.zeros((head_count, row_count), jnp.float32),
        jnp.zeros((head_count, row_count, DH), jnp.float32),
    )
    queries = q_soft.reshape(query_shape)
    query_pos = my_index * row_count + positions
    query_end = my_index * row_count + row_count - 1

    def visitor(running, keys_here, values_here, block_start):
        return lax.cond(
            block_start <= query_end,
            lambda state: soft_update(
                state,
                queries,
                query_pos,
                keys_here.reshape(key_shape),
                values_here.reshape(key_shape),
                block_start + positions,
            ),
            lambda state: state,
            running,
        )

    row_max, row_total, weighted = over_blocks(
        initial,
        (
            lax.all_gather(k_local, "ctx", axis=0, tiled=True),
            lax.all_gather(v_local, "ctx", axis=0, tiled=True),
        ),
        row_count,
        visitor,
    )
    soft_out = finish(row_total, weighted, row_count, width)
    return (linear_out, soft_out)


def solution(mesh):
    return jax.shard_map(
        local,
        mesh=mesh,
        in_specs=(
            P("ctx", "head"),
            P("ctx", "head"),
            P("ctx", "head"),
            P("ctx", "head"),
            P("head"),
            P("ctx", "head"),
            P("ctx", None),
            P("ctx", None),
        ),
        out_specs=(P("ctx", "head"), P("ctx", "head")),
        check_vma=False,
    )
```

profile of v0, /device:TPU:6, one launch (start us, length us, event | category | flops | bytes accessed | tf_op | source)
XLA Modules:
  0.0 451.1 jit_solution(13501809953526398341)
XLA Ops:
  16.4 310.2 %while.9 = (s32[]{:T(128)}, f32[4,128,128]{2,1,0:T(8,128)S(1)}, f32[4]{0:T(128)S(1)}, f32[4,128,128]{2,1,0:T(8,128)S(1)}, s32[]{:T(128)}) while((s32[]{:T(128)}, f32[4,128,128]{2,1,0:T(8,128)S(1)}, f32[4]{0:T(128)S(1)}, f32[4,128,128]{2,1,0:T(8,128)S(1)}, s32[]{:T(128)}) %tuple.85), condition=%wide.region_3.4_spmd, body=%wide.region_2.3_spmd.sunk | while | flops 131074 | bytes 1835125 | solution.py:112
  18.5 7.9 %collective-permute-done = f32[4,128,128]{2,1,0:T(8,128)S(1)} collective-permute-done((f32[4,128,128]{2,1,0:T(8,128)S(1)}, f32[4,128,128]{2,1,0:T(8,128)S(1)}, u32[]{:S(2)}, u32[]{:S(2)}) %collective-permute-start) | collective-permute-done | bytes 262176 | tf_op jit(solution)/shard_map/while/body/eval_jaxpr/ppermute | solution.py:17
  26.4 1.9 collective-permute-start
  28.4 7.9 %collective-permute-done = f32[4,128,128]{2,1,0:T(8,128)S(1)} collective-permute-done((f32[4,128,128]{2,1,0:T(8,128)S(1)}, f32[4,128,128]{2,1,0:T(8,128)S(1)}, u32[]{:S(2)}, u32[]{:S(2)}) %collective-permute-start) | collective-permute-done | bytes 262176 | tf_op jit(solution)/shard_map/while/body/eval_jaxpr/ppermute | solution.py:17
  38.3 8.0 %collective-permute-done = f32[4,128,128]{2,1,0:T(8,128)S(1)} collective-permute-done((f32[4,128,128]{2,1,0:T(8,128)S(1)}, f32[4,128,128]{2,1,0:T(8,128)S(1)}, u32[]{:S(2)}, u32[]{:S(2)}) %collective-permute-start) | collective-permute-done | bytes 262176 | tf_op jit(solution)/shard_map/while/body/eval_jaxpr/ppermute | solution.py:17
  46.4 1.9 collective-permute-start
  48.3 7.9 %collective-permute-done = f32[4,128,128]{2,1,0:T(8,128)S(1)} collective-permute-done((f32[4,128,128]{2,1,0:T(8,128)S(1)}, f32[4,128,128]{2,1,0:T(8,128)S(1)}, u32[]{:S(2)}, u32[]{:S(2)}) %collective-permute-start) | collective-permute-done | bytes 262176 | tf_op jit(solution)/shard_map/while/body/eval_jaxpr/ppermute | solution.py:17
  56.3 1.9 collective-permute-start
  58.2 8.4 %collective-permute-done = f32[4,128,128]{2,1,0:T(8,128)S(1)} collective-permute-done((f32[4,128,128]{2,1,0:T(8,128)S(1)}, f32[4,128,128]{2,1,0:T(8,128)S(1)}, u32[]{:S(2)}, u32[]{:S(2)}) %collective-permute-start) | collective-permute-done | bytes 262176 | tf_op jit(solution)/shard_map/while/body/eval_jaxpr/ppermute | solution.py:17
  68.6 8.7 %collective-permute-done = f32[4,128,128]{2,1,0:T(8,128)S(1)} collective-permute-done((f32[4,128,128]{2,1,0:T(8,128)S(1)}, f32[4,128,128]{2,1,0:T(8,128)S(1)}, u32[]{:S(2)}, u32[]{:S(2)}) %collective-permute-start) | collective-permute-done | bytes 262176 | tf_op jit(solution)/shard_map/while/body/eval_jaxpr/ppermute | solution.py:17
  79.4 7.9 %collective-permute-done = f32[4,128,128]{2,1,0:T(8,128)S(1)} collective-permute-done((f32[4,128,128]{2,1,0:T(8,128)S(1)}, f32[4,128,128]{2,1,0:T(8,128)S(1)}, u32[]{:S(2)}, u32[]{:S(2)}) %collective-permute-start) | collective-permute-done | bytes 262176 | tf_op jit(solution)/shard_map/while/body/eval_jaxpr/ppermute | solution.py:17
  87.4 1.9 collective-permute-start
  89.3 7.9 %collective-permute-done = f32[4,128,128]{2,1,0:T(8,128)S(1)} collective-permute-done((f32[4,128,128]{2,1,0:T(8,128)S(1)}, f32[4,128,128]{2,1,0:T(8,128)S(1)}, u32[]{:S(2)}, u32[]{:S(2)}) %collective-permute-start) | collective-permute-done | bytes 262176 | tf_op jit(solution)/shard_map/while/body/eval_jaxpr/ppermute | solution.py:17
  99.2 8.3 %collective-permute-done = f32[4,128,128]{2,1,0:T(8,128)S(1)} collective-permute-done((f32[4,128,128]{2,1,0:T(8,128)S(1)}, f32[4,128,128]{2,1,0:T(8,128)S(1)}, u32[]{:S(2)}, u32[]{:S(2)}) %collective-permute-start) | collective-permute-done | bytes 262176 | tf_op jit(solution)/shard_map/while/body/eval_jaxpr/ppermute | solution.py:17
  107.6 1.9 collective-permute-start
  109.5 7.9 %collective-permute-done = f32[4,128,128]{2,1,0:T(8,128)S(1)} collective-permute-done((f32[4,128,128]{2,1,0:T(8,128)S(1)}, f32[4,128,128]{2,1,0:T(8,128)S(1)}, u32[]{:S(2)}, u32[]{:S(2)}) %collective-permute-start) | collective-permute-done | bytes 262176 | tf_op jit(solution)/shard_map/while/body/eval_jaxpr/ppermute | solution.py:17
  119.4 7.9 %collective-permute-done = f32[4,128,128]{2,1,0:T(8,128)S(1)} collective-permute-done((f32[4,128,128]{2,1,0:T(8,128)S(1)}, f32[4,128,128]{2,1,0:T(8,128)S(1)}, u32[]{:S(2)}, u32[]{:S(2)}) %collective-permute-start) | collective-permute-done | bytes 262176 | tf_op jit(solution)/shard_map/while/body/eval_jaxpr/ppermute | solution.py:17
  129.3 9.3 %collective-permute-done = f32[4,128,128]{2,1,0:T(8,128)S(1)} collective-permute-done((f32[4,128,128]{2,1,0:T(8,128)S(1)}, f32[4,128,128]{2,1,0:T(8,128)S(1)}, u32[]{:S(2)}, u32[]{:S(2)}) %collective-permute-start) | collective-permute-done | bytes 262176 | tf_op jit(solution)/shard_map/while/body/eval_jaxpr/ppermute | solution.py:17
  140.6 7.9 %collective-permute-done = f32[4,128,128]{2,1,0:T(8,128)S(1)} collective-permute-done((f32[4,128,128]{2,1,0:T(8,128)S(1)}, f32[4,128,128]{2,1,0:T(8,128)S(1)}, u32[]{:S(2)}, u32[]{:S(2)}) %collective-permute-start) | collective-permute-done | bytes 262176 | tf_op jit(solution)/shard_map/while/body/eval_jaxpr/ppermute | solution.py:17
  150.5 7.9 %collective-permute-done = f32[4,128,128]{2,1,0:T(8,128)S(1)} collective-permute-done((f32[4,128,128]{2,1,0:T(8,128)S(1)}, f32[4,128,128]{2,1,0:T(8,128)S(1)}, u32[]{:S(2)}, u32[]{:S(2)}) %collective-permute-start) | collective-permute-done | bytes 262176 | tf_op jit(solution)/shard_map/while/body/eval_jaxpr/ppermute | solution.py:17
  160.4 7.9 %collective-permute-done = f32[4,128,128]{2,1,0:T(8,128)S(1)} collective-permute-done((f32[4,128,128]{2,1,0:T(8,128)S(1)}, f32[4,128,128]{2,1,0:T(8,128)S(1)}, u32[]{:S(2)}, u32[]{:S(2)}) %collective-permute-start) | collective-permute-done | bytes 262176 | tf_op jit(solution)/shard_map/while/body/eval_jaxpr/ppermute | solution.py:17
  170.3 7.9 %collective-permute-done = f32[4,128,128]{2,1,0:T(8,128)S(1)} collective-permute-done((f32[4,128,128]{2,1,0:T(8,128)S(1)}, f32[4,128,128]{2,1,0:T(8,128)S(1)}, u32[]{:S(2)}, u32[]{:S(2)}) %collective-permute-start) | collective-permute-done | bytes 262176 | tf_op jit(solution)/shard_map/while/body/eval_jaxpr/ppermute | solution.py:17
  180.2 7.9 %collective-permute-done = f32[4,128,128]{2,1,0:T(8,128)S(1)} collective-permute-done((f32[4,128,128]{2,1,0:T(8,128)S(1)}, f32[4,128,128]{2,1,0:T(8,128)S(1)}, u32[]{:S(2)}, u32[]{:S(2)}) %collective-permute-start) | collective-permute-done | bytes 262176 | tf_op jit(solution)/shard_map/while/body/eval_jaxpr/ppermute | solution.py:17
  190.1 7.9 %collective-permute-done = f32[4,128,128]{2,1,0:T(8,128)S(1)} collective-permute-done((f32[4,128,128]{2,1,0:T(8,128)S(1)}, f32[4,128,128]{2,1,0:T(8,128)S(1)}, u32[]{:S(2)}, u32[]{:S(2)}) %collective-permute-start) | collective-permute-done | bytes 262176 | tf_op jit(solution)/shard_map/while/body/eval_jaxpr/ppermute | solution.py:17
  200.0 7.9 %collective-permute-done = f32[4,128,128]{2,1,0:T(8,128)S(1)} collective-permute-done((f32[4,128,128]{2,1,0:T(8,128)S(1)}, f32[4,128,128]{2,1,0:T(8,128)S(1)}, u32[]{:S(2)}, u32[]{:S(2)}) %collective-permute-start) | collective-permute-done | bytes 262176 | tf_op jit(solution)/shard_map/while/body/eval_jaxpr/ppermute | solution.py:17
  209.9 7.9 %collective-permute-done = f32[4,128,128]{2,1,0:T(8,128)S(1)} collective-permute-done((f32[4,128,128]{2,1,0:T(8,128)S(1)}, f32[4,128,128]{2,1,0:T(8,128)S(1)}, u32[]{:S(2)}, u32[]{:S(2)}) %collective-permute-start) | collective-permute-done | bytes 262176 | tf_op jit(solution)/shard_map/while/body/eval_jaxpr/ppermute | solution.py:17
  219.8 7.9 %collective-permute-done = f32[4,128,128]{2,1,0:T(8,128)S(1)} collective-permute-done((f32[4,128,128]{2,1,0:T(8,128)S(1)}, f32[4,128,128]{2,1,0:T(8,128)S(1)}, u32[]{:S(2)}, u32[]{:S(2)}) %collective-permute-start) | collective-permute-done | bytes 262176 | tf_op jit(solution)/shard_map/while/body/eval_jaxpr/ppermute | solution.py:17
  229.7 7.9 %collective-permute-done = f32[4,128,128]{2,1,0:T(8,128)S(1)} collective-permute-done((f32[4,128,128]{2,1,0:T(8,128)S(1)}, f32[4,128,128]{2,1,0:T(8,128)S(1)}, u32[]{:S(2)}, u32[]{:S(2)}) %collective-permute-start) | collective-permute-done | bytes 262176 | tf_op jit(solution)/shard_map/while/body/eval_jaxpr/ppermute | solution.py:17
  239.6 7.9 %collective-permute-done = f32[4,128,128]{2,1,0:T(8,128)S(1)} collective-permute-done((f32[4,128,128]{2,1,0:T(8,128)S(1)}, f32[4,128,128]{2,1,0:T(8,128)S(1)}, u32[]{:S(2)}, u32[]{:S(2)}) %collective-permute-start) | collective-permute-done | bytes 262176 | tf_op jit(solution)/shard_map/while/body/eval_jaxpr/ppermute | solution.py:17
  249.5 7.9 %collective-permute-done = f32[4,128,128]{2,1,0:T(8,128)S(1)} collective-permute-done((f32[4,128,128]{2,1,0:T(8,128)S(1)}, f32[4,128,128]{2,1,0:T(8,128)S(1)}, u32[]{:S(2)}, u32[]{:S(2)}) %collective-permute-start) | collective-permute-done | bytes 262176 | tf_op jit(solution)/shard_map/while/body/eval_jaxpr/ppermute | solution.py:17
  259.4 7.9 %collective-permute-done = f32[4,128,128]{2,1,0:T(8,128)S(1)} collective-permute-done((f32[4,128,128]{2,1,0:T(8,128)S(1)}, f32[4,128,128]{2,1,0:T(8,128)S(1)}, u32[]{:S(2)}, u32[]{:S(2)}) %collective-permute-start) | collective-permute-done | bytes 262176 | tf_op jit(solution)/shard_map/while/body/eval_jaxpr/ppermute | solution.py:17
  269.3 7.9 %collective-permute-done = f32[4,128,128]{2,1,0:T(8,128)S(1)} collective-permute-done((f32[4,128,128]{2,1,0:T(8,128)S(1)}, f32[4,128,128]{2,1,0:T(8,128)S(1)}, u32[]{:S(2)}, u32[]{:S(2)}) %collective-permute-start) | collective-permute-done | bytes 262176 | tf_op jit(solution)/shard_map/while/body/eval_jaxpr/ppermute | solution.py:17
  279.2 7.9 %collective-permute-done = f32[4,128,128]{2,1,0:T(8,128)S(1)} collective-permute-done((f32[4,128,128]{2,1,0:T(8,128)S(1)}, f32[4,128,128]{2,1,0:T(8,128)S(1)}, u32[]{:S(2)}, u32[]{:S(2)}) %collective-permute-start) | collective-permute-done | bytes 262176 | tf_op jit(solution)/shard_map/while/body/eval_jaxpr/ppermute | solution.py:17
  289.1 7.9 %collective-permute-done = f32[4,128,128]{2,1,0:T(8,128)S(1)} collective-permute-done((f32[4,128,128]{2,1,0:T(8,128)S(1)}, f32[4,128,128]{2,1,0:T(8,128)S(1)}, u32[]{:S(2)}, u32[]{:S(2)}) %collective-permute-start) | collective-permute-done | bytes 262176 | tf_op jit(solution)/shard_map/while/body/eval_jaxpr/ppermute | solution.py:17
  299.0 7.9 %collective-permute-done = f32[4,128,128]{2,1,0:T(8,128)S(1)} collective-permute-done((f32[4,128,128]{2,1,0:T(8,128)S(1)}, f32[4,128,128]{2,1,0:T(8,128)S(1)}, u32[]{:S(2)}, u32[]{:S(2)}) %collective-permute-start) | collective-permute-done | bytes 262176 | tf_op jit(solution)/shard_map/while/body/eval_jaxpr/ppermute | solution.py:17
  308.9 7.9 %collective-permute-done = f32[4,128,128]{2,1,0:T(8,128)S(1)} collective-permute-done((f32[4,128,128]{2,1,0:T(8,128)S(1)}, f32[4,128,128]{2,1,0:T(8,128)S(1)}, u32[]{:S(2)}, u32[]{:S(2)}) %collective-permute-start) | collective-permute-done | bytes 262176 | tf_op jit(solution)/shard_map/while/body/eval_jaxpr/ppermute | solution.py:17
  318.8 7.9 %collective-permute-done = f32[4,128,128]{2,1,0:T(8,128)S(1)} collective-permute-done((f32[4,128,128]{2,1,0:T(8,128)S(1)}, f32[4,128,128]{2,1,0:T(8,128)S(1)}, u32[]{:S(2)}, u32[]{:S(2)}) %collective-permute-start) | collective-permute-done | bytes 262176 | tf_op jit(solution)/shard_map/while/body/eval_jaxpr/ppermute | solution.py:17
  328.2 37.5 %psum.7 = f32[256]{0:T(256)S(1)} all-reduce(f32[256]{0:T(256)S(1)} %get-tuple-element.439), channel_id=1, replica_groups=mesh['ctx'=32,'head'=16] {'head'}, use_global_device_ids=true, to_apply=%region_5.6 | all-reduce | flops 256 | bytes 2048 | tf_op jit(solution)/shard_map/psum | solution.py:115
  366.6 76.8 %while.36 = (s32[]{:T(128)}, f32[4,256]{1,0:T(4,128)S(1)}, f32[4,256]{1,0:T(4,128)S(1)}, f32[4,256,128]{2,1,0:T(8,128)S(1)}, s32[]{:T(128)}, /*index=5*/bf16[819...) while((s32[]{:T(128)}, f32[4,256]{1,0:T(4,128)S(1)}, ...), condition=%wide.region_11.12_spmd.clone, body=%wide.region_6.11_spmd.clone.sunk | while | flops 137431552 | bytes 4922689 | solution.py:74
  366.6 3.0 conditional.3
  369.7 3.0 conditional.3
  372.7 3.0 conditional.3
  375.8 3.0 conditional.3
  378.8 3.0 conditional.3
  381.9 3.0 conditional.3
  384.9 3.0 conditional.3
  388.0 3.0 conditional.3
  391.1 3.0 conditional.3
  394.1 3.0 conditional.3
  397.2 3.0 conditional.3
  400.2 3.0 conditional.3
  403.3 3.0 conditional.3
  406.3 3.0 conditional.3
  409.4 3.0 conditional.3
  412.5 3.0 conditional.3
  415.5 3.0 conditional.3
  418.6 3.0 conditional.3
  421.6 3.0 conditional.3
  424.7 3.0 conditional.3
  427.7 3.0 conditional.3
  430.8 3.0 conditional.3
  433.9 3.0 conditional.3
  436.9 3.0 conditional.3
  440.0 3.0 conditional.3
  (340 shorter events, 139.1 us)
Async XLA Ops:
  7.2 1.0 copy-start
  7.2 8.2 %copy-start.1 = (bf16[256,512]{1,0:T(8,128)(2,1)S(1)}, bf16[256,512]{1,0:T(8,128)(2,1)}, u32[]{:S(2)}) copy-start(bf16[256,512]{1,0:T(8,128)(2,1)} %param.14) | copy-start | bytes 786436
  7.2 9.0 %copy-start.2 = (bf16[256,512]{1,0:T(8,128)(2,1)S(1)}, bf16[256,512]{1,0:T(8,128)(2,1)}, u32[]{:S(2)}) copy-start(bf16[256,512]{1,0:T(8,128)(2,1)} %param.16) | copy-start | bytes 786436
  7.2 359.3 %all-gather.3.cloned.1.call-start = ((), (), s32[]{:S(2)}) async-start(), calls=%async_computation | async-start | bytes 2162688 | tf_op jit(solution)/shard_map/all_gather | solution.py:156
  8.9 357.6 %all-gather.5.cloned.1.call-start = ((), (), s32[]{:S(2)}) async-start(), calls=%async_computation.1 | async-start | bytes 2162688 | tf_op jit(solution)/shard_map/all_gather | solution.py:157
  16.5 9.8 %collective-permute-start = (f32[4,128,128]{2,1,0:T(8,128)S(1)}, f32[4,128,128]{2,1,0:T(8,128)S(1)}, u32[]{:S(2)}, u32[]{:S(2)}) collective-permute-start(f32[4,128,128]{2,1,0:T(8,128)S(1)} %multiply_add_fusion.3), channel_id=1, source_target_pairs={{0,16},{16,32},{32,48},{48,64},{64,80},{80,96},{96,112},{112,128},... | collective-permute-start | bytes 786440 | tf_op jit(solution)/shard_map/while/body/eval_jaxpr/ppermute | solution.py:17
  26.4 9.8 %collective-permute-start = (f32[4,128,128]{2,1,0:T(8,128)S(1)}, f32[4,128,128]{2,1,0:T(8,128)S(1)}, u32[]{:S(2)}, u32[]{:S(2)}) collective-permute-start(f32[4,128,128]{2,1,0:T(8,128)S(1)} %multiply_add_fusion.3), channel_id=1, source_target_pairs={{0,16},{16,32},{32,48},{48,64},{64,80},{80,96},{96,112},{112,128},... | collective-permute-start | bytes 786440 | tf_op jit(solution)/shard_map/while/body/eval_jaxpr/ppermute | solution.py:17
  36.3 10.0 %collective-permute-start = (f32[4,128,128]{2,1,0:T(8,128)S(1)}, f32[4,128,128]{2,1,0:T(8,128)S(1)}, u32[]{:S(2)}, u32[]{:S(2)}) collective-permute-start(f32[4,128,128]{2,1,0:T(8,128)S(1)} %multiply_add_fusion.3), channel_id=1, source_target_pairs={{0,16},{16,32},{32,48},{48,64},{64,80},{80,96},{96,112},{112,128},... | collective-permute-start | bytes 786440 | tf_op jit(solution)/shard_map/while/body/eval_jaxpr/ppermute | solution.py:17
  46.4 9.8 %collective-permute-start = (f32[4,128,128]{2,1,0:T(8,128)S(1)}, f32[4,128,128]{2,1,0:T(8,128)S(1)}, u32[]{:S(2)}, u32[]{:S(2)}) collective-permute-start(f32[4,128,128]{2,1,0:T(8,128)S(1)} %multiply_add_fusion.3), channel_id=1, source_target_pairs={{0,16},{16,32},{32,48},{48,64},{64,80},{80,96},{96,112},{112,128},... | collective-permute-start | bytes 786440 | tf_op jit(solution)/shard_map/while/body/eval_jaxpr/ppermute | solution.py:17
  56.3 10.3 %collective-permute-start = (f32[4,128,128]{2,1,0:T(8,128)S(1)}, f32[4,128,128]{2,1,0:T(8,128)S(1)}, u32[]{:S(2)}, u32[]{:S(2)}) collective-permute-start(f32[4,128,128]{2,1,0:T(8,128)S(1)} %multiply_add_fusion.3), channel_id=1, source_target_pairs={{0,16},{16,32},{32,48},{48,64},{64,80},{80,96},{96,112},{112,128},... | collective-permute-start | bytes 786440 | tf_op jit(solution)/shard_map/while/body/eval_jaxpr/ppermute | solution.py:17
  66.7 10.7 %collective-permute-start = (f32[4,128,128]{2,1,0:T(8,128)S(1)}, f32[4,128,128]{2,1,0:T(8,128)S(1)}, u32[]{:S(2)}, u32[]{:S(2)}) collective-permute-start(f32[4,128,128]{2,1,0:T(8,128)S(1)} %multiply_add_fusion.3), channel_id=1, source_target_pairs={{0,16},{16,32},{32,48},{48,64},{64,80},{80,96},{96,112},{112,128},... | collective-permute-start | bytes 786440 | tf_op jit(solution)/shard_map/while/body/eval_jaxpr/ppermute | solution.py:17
  77.5 9.8 %collective-permute-start = (f32[4,128,128]{2,1,0:T(8,128)S(1)}, f32[4,128,128]{2,1,0:T(8,128)S(1)}, u32[]{:S(2)}, u32[]{:S(2)}) collective-permute-start(f32[4,128,128]{2,1,0:T(8,128)S(1)} %multiply_add_fusion.3), channel_id=1, source_target_pairs={{0,16},{16,32},{32,48},{48,64},{64,80},{80,96},{96,112},{112,128},... | collective-permute-start | bytes 786440 | tf_op jit(solution)/shard_map/while/body/eval_jaxpr/ppermute | solution.py:17
  87.4 9.8 %collective-permute-start = (f32[4,128,128]{2,1,0:T(8,128)S(1)}, f32[4,128,128]{2,1,0:T(8,128)S(1)}, u32[]{:S(2)}, u32[]{:S(2)}) collective-permute-start(f32[4,128,128]{2,1,0:T(8,128)S(1)} %multiply_add_fusion.3), channel_id=1, source_target_pairs={{0,16},{16,32},{32,48},{48,64},{64,80},{80,96},{96,112},{112,128},... | collective-permute-start | bytes 786440 | tf_op jit(solution)/shard_map/while/body/eval_jaxpr/ppermute | solution.py:17
  97.3 10.2 %collective-permute-start = (f32[4,128,128]{2,1,0:T(8,128)S(1)}, f32[4,128,128]{2,1,0:T(8,128)S(1)}, u32[]{:S(2)}, u32[]{:S(2)}) collective-permute-start(f32[4,128,128]{2,1,0:T(8,128)S(1)} %multiply_add_fusion.3), channel_id=1, source_target_pairs={{0,16},{16,32},{32,48},{48,64},{64,80},{80,96},{96,112},{112,128},... | collective-permute-start | bytes 786440 | tf_op jit(solution)/shard_map/while/body/eval_jaxpr/ppermute | solution.py:17
  107.6 9.8 %collective-permute-start = (f32[4,128,128]{2,1,0:T(8,128)S(1)}, f32[4,128,128]{2,1,0:T(8,128)S(1)}, u32[]{:S(2)}, u32[]{:S(2)}) collective-permute-start(f32[4,128,128]{2,1,0:T(8,128)S(1)} %multiply_add_fusion.3), channel_id=1, source_target_pairs={{0,16},{16,32},{32,48},{48,64},{64,80},{80,96},{96,112},{112,128},... | collective-permute-start | bytes 786440 | tf_op jit(solution)/shard_map/while/body/eval_jaxpr/ppermute | solution.py:17
  117.5 9.8 %collective-permute-start = (f32[4,128,128]{2,1,0:T(8,128)S(1)}, f32[4,128,128]{2,1,0:T(8,128)S(1)}, u32[]{:S(2)}, u32[]{:S(2)}) collective-permute-start(f32[4,128,128]{2,1,0:T(8,128)S(1)} %multiply_add_fusion.3), channel_id=1, source_target_pairs={{0,16},{16,32},{32,48},{48,64},{64,80},{80,96},{96,112},{112,128},... | collective-permute-start | bytes 786440 | tf_op jit(solution)/shard_map/while/body/eval_jaxpr/ppermute | solution.py:17
  127.4 11.2 %collective-permute-start = (f32[4,128,128]{2,1,0:T(8,128)S(1)}, f32[4,128,128]{2,1,0:T(8,128)S(1)}, u32[]{:S(2)}, u32[]{:S(2)}) collective-permute-start(f32[4,128,128]{2,1,0:T(8,128)S(1)} %multiply_add_fusion.3), channel_id=1, source_target_pairs={{0,16},{16,32},{32,48},{48,64},{64,80},{80,96},{96,112},{112,128},... | collective-permute-start | bytes 786440 | tf_op jit(solution)/shard_map/while/body/eval_jaxpr/ppermute | solution.py:17
  138.7 9.8 %collective-permute-start = (f32[4,128,128]{2,1,0:T(8,128)S(1)}, f32[4,128,128]{2,1,0:T(8,128)S(1)}, u32[]{:S(2)}, u32[]{:S(2)}) collective-permute-start(f32[4,128,128]{2,1,0:T(8,128)S(1)} %multiply_add_fusion.3), channel_id=1, source_target_pairs={{0,16},{16,32},{32,48},{48,64},{64,80},{80,96},{96,112},{112,128},... | collective-permute-start | bytes 786440 | tf_op jit(solution)/shard_map/while/body/eval_jaxpr/ppermute | solution.py:17
  148.6 9.8 %collective-permute-start = (f32[4,128,128]{2,1,0:T(8,128)S(1)}, f32[4,128,128]{2,1,0:T(8,128)S(1)}, u32[]{:S(2)}, u32[]{:S(2)}) collective-permute-start(f32[4,128,128]{2,1,0:T(8,128)S(1)} %multiply_add_fusion.3), channel_id=1, source_target_pairs={{0,16},{16,32},{32,48},{48,64},{64,80},{80,96},{96,112},{112,128},... | collective-permute-start | bytes 786440 | tf_op jit(solution)/shard_map/while/body/eval_jaxpr/ppermute | solution.py:17
  158.5 9.8 %collective-permute-start = (f32[4,128,128]{2,1,0:T(8,128)S(1)}, f32[4,128,128]{2,1,0:T(8,128)S(1)}, u32[]{:S(2)}, u32[]{:S(2)}) collective-permute-start(f32[4,128,128]{2,1,0:T(8,128)S(1)} %multiply_add_fusion.3), channel_id=1, source_target_pairs={{0,16},{16,32},{32,48},{48,64},{64,80},{80,96},{96,112},{112,128},... | collective-permute-start | bytes 786440 | tf_op jit(solution)/shard_map/while/body/eval_jaxpr/ppermute | solution.py:17
  168.4 9.8 %collective-permute-start = (f32[4,128,128]{2,1,0:T(8,128)S(1)}, f32[4,128,128]{2,1,0:T(8,128)S(1)}, u32[]{:S(2)}, u32[]{:S(2)}) collective-permute-start(f32[4,128,128]{2,1,0:T(8,128)S(1)} %multiply_add_fusion.3), channel_id=1, source_target_pairs={{0,16},{16,32},{32,48},{48,64},{64,80},{80,96},{96,112},{112,128},... | collective-permute-start | bytes 786440 | tf_op jit(solution)/shard_map/while/body/eval_jaxpr/ppermute | solution.py:17
  178.3 9.8 %collective-permute-start = (f32[4,128,128]{2,1,0:T(8,128)S(1)}, f32[4,128,128]{2,1,0:T(8,128)S(1)}, u32[]{:S(2)}, u32[]{:S(2)}) collective-permute-start(f32[4,128,128]{2,1,0:T(8,128)S(1)} %multiply_add_fusion.3), channel_id=1, source_target_pairs={{0,16},{16,32},{32,48},{48,64},{64,80},{80,96},{96,112},{112,128},... | collective-permute-start | bytes 786440 | tf_op jit(solution)/shard_map/while/body/eval_jaxpr/ppermute | solution.py:17
  188.2 9.8 %collective-permute-start = (f32[4,128,128]{2,1,0:T(8,128)S(1)}, f32[4,128,128]{2,1,0:T(8,128)S(1)}, u32[]{:S(2)}, u32[]{:S(2)}) collective-permute-start(f32[4,128,128]{2,1,0:T(8,128)S(1)} %multiply_add_fusion.3), channel_id=1, source_target_pairs={{0,16},{16,32},{32,48},{48,64},{64,80},{80,96},{96,112},{112,128},... | collective-permute-start | bytes 786440 | tf_op jit(solution)/shard_map/while/body/eval_jaxpr/ppermute | solution.py:17
  198.1 9.8 %collective-permute-start = (f32[4,128,128]{2,1,0:T(8,128)S(1)}, f32[4,128,128]{2,1,0:T(8,128)S(1)}, u32[]{:S(2)}, u32[]{:S(2)}) collective-permute-start(f32[4,128,128]{2,1,0:T(8,128)S(1)} %multiply_add_fusion.3), channel_id=1, source_target_pairs={{0,16},{16,32},{32,48},{48,64},{64,80},{80,96},{96,112},{112,128},... | collective-permute-start | bytes 786440 | tf_op jit(solution)/shard_map/while/body/eval_jaxpr/ppermute | solution.py:17
  208.0 9.8 %collective-permute-start = (f32[4,128,128]{2,1,0:T(8,128)S(1)}, f32[4,128,128]{2,1,0:T(8,128)S(1)}, u32[]{:S(2)}, u32[]{:S(2)}) collective-permute-start(f32[4,128,128]{2,1,0:T(8,128)S(1)} %multiply_add_fusion.3), channel_id=1, source_target_pairs={{0,16},{16,32},{32,48},{48,64},{64,80},{80,96},{96,112},{112,128},... | collective-permute-start | bytes 786440 | tf_op jit(solution)/shard_map/while/body/eval_jaxpr/ppermute | solution.py:17
  217.9 9.8 %collective-permute-start = (f32[4,128,128]{2,1,0:T(8,128)S(1)}, f32[4,128,128]{2,1,0:T(8,128)S(1)}, u32[]{:S(2)}, u32[]{:S(2)}) collective-permute-start(f32[4,128,128]{2,1,0:T(8,128)S(1)} %multiply_add_fusion.3), channel_id=1, source_target_pairs={{0,16},{16,32},{32,48},{48,64},{64,80},{80,96},{96,112},{112,128},... | collective-permute-start | bytes 786440 | tf_op jit(solution)/shard_map/while/body/eval_jaxpr/ppermute | solution.py:17
  227.8 9.8 %collective-permute-start = (f32[4,128,128]{2,1,0:T(8,128)S(1)}, f32[4,128,128]{2,1,0:T(8,128)S(1)}, u32[]{:S(2)}, u32[]{:S(2)}) collective-permute-start(f32[4,128,128]{2,1,0:T(8,128)S(1)} %multiply_add_fusion.3), channel_id=1, source_target_pairs={{0,16},{16,32},{32,48},{48,64},{64,80},{80,96},{96,112},{112,128},... | collective-permute-start | bytes 786440 | tf_op jit(solution)/shard_map/while/body/eval_jaxpr/ppermute | solution.py:17
  237.7 9.8 %collective-permute-start = (f32[4,128,128]{2,1,0:T(8,128)S(1)}, f32[4,128,128]{2,1,0:T(8,128)S(1)}, u32[]{:S(2)}, u32[]{:S(2)}) collective-permute-start(f32[4,128,128]{2,1,0:T(8,128)S(1)} %multiply_add_fusion.3), channel_id=1, source_target_pairs={{0,16},{16,32},{32,48},{48,64},{64,80},{80,96},{96,112},{112,128},... | collective-permute-start | bytes 786440 | tf_op jit(solution)/shard_map/while/body/eval_jaxpr/ppermute | solution.py:17
  247.5 9.8 %collective-permute-start = (f32[4,128,128]{2,1,0:T(8,128)S(1)}, f32[4,128,128]{2,1,0:T(8,128)S(1)}, u32[]{:S(2)}, u32[]{:S(2)}) collective-permute-start(f32[4,128,128]{2,1,0:T(8,128)S(1)} %multiply_add_fusion.3), channel_id=1, source_target_pairs={{0,16},{16,32},{32,48},{48,64},{64,80},{80,96},{96,112},{112,128},... | collective-permute-start | bytes 786440 | tf_op jit(solution)/shard_map/while/body/eval_jaxpr/ppermute | solution.py:17
  257.4 9.8 %collective-permute-start = (f32[4,128,128]{2,1,0:T(8,128)S(1)}, f32[4,128,128]{2,1,0:T(8,128)S(1)}, u32[]{:S(2)}, u32[]{:S(2)}) collective-permute-start(f32[4,128,128]{2,1,0:T(8,128)S(1)} %multiply_add_fusion.3), channel_id=1, source_target_pairs={{0,16},{16,32},{32,48},{48,64},{64,80},{80,96},{96,112},{112,128},... | collective-permute-start | bytes 786440 | tf_op jit(solution)/shard_map/while/body/eval_jaxpr/ppermute | solution.py:17
  267.3 9.8 %collective-permute-start = (f32[4,128,128]{2,1,0:T(8,128)S(1)}, f32[4,128,128]{2,1,0:T(8,128)S(1)}, u32[]{:S(2)}, u32[]{:S(2)}) collective-permute-start(f32[4,128,128]{2,1,0:T(8,128)S(1)} %multiply_add_fusion.3), channel_id=1, source_target_pairs={{0,16},{16,32},{32,48},{48,64},{64,80},{80,96},{96,112},{112,128},... | collective-permute-start | bytes 786440 | tf_op jit(solution)/shard_map/while/body/eval_jaxpr/ppermute | solution.py:17
  277.2 9.8 %collective-permute-start = (f32[4,128,128]{2,1,0:T(8,128)S(1)}, f32[4,128,128]{2,1,0:T(8,128)S(1)}, u32[]{:S(2)}, u32[]{:S(2)}) collective-permute-start(f32[4,128,128]{2,1,0:T(8,128)S(1)} %multiply_add_fusion.3), channel_id=1, source_target_pairs={{0,16},{16,32},{32,48},{48,64},{64,80},{80,96},{96,112},{112,128},... | collective-permute-start | bytes 786440 | tf_op jit(solution)/shard_map/while/body/eval_jaxpr/ppermute | solution.py:17
  287.1 9.8 %collective-permute-start = (f32[4,128,128]{2,1,0:T(8,128)S(1)}, f32[4,128,128]{2,1,0:T(8,128)S(1)}, u32[]{:S(2)}, u32[]{:S(2)}) collective-permute-start(f32[4,128,128]{2,1,0:T(8,128)S(1)} %multiply_add_fusion.3), channel_id=1, source_target_pairs={{0,16},{16,32},{32,48},{48,64},{64,80},{80,96},{96,112},{112,128},... | collective-permute-start | bytes 786440 | tf_op jit(solution)/shard_map/while/body/eval_jaxpr/ppermute | solution.py:17
  297.0 9.8 %collective-permute-start = (f32[4,128,128]{2,1,0:T(8,128)S(1)}, f32[4,128,128]{2,1,0:T(8,128)S(1)}, u32[]{:S(2)}, u32[]{:S(2)}) collective-permute-start(f32[4,128,128]{2,1,0:T(8,128)S(1)} %multiply_add_fusion.3), channel_id=1, source_target_pairs={{0,16},{16,32},{32,48},{48,64},{64,80},{80,96},{96,112},{112,128},... | collective-permute-start | bytes 786440 | tf_op jit(solution)/shard_map/while/body/eval_jaxpr/ppermute | solution.py:17
  306.9 9.8 %collective-permute-start = (f32[4,128,128]{2,1,0:T(8,128)S(1)}, f32[4,128,128]{2,1,0:T(8,128)S(1)}, u32[]{:S(2)}, u32[]{:S(2)}) collective-permute-start(f32[4,128,128]{2,1,0:T(8,128)S(1)} %multiply_add_fusion.3), channel_id=1, source_target_pairs={{0,16},{16,32},{32,48},{48,64},{64,80},{80,96},{96,112},{112,128},... | collective-permute-start | bytes 786440 | tf_op jit(solution)/shard_map/while/body/eval_jaxpr/ppermute | solution.py:17
  316.8 9.8 %collective-permute-start = (f32[4,128,128]{2,1,0:T(8,128)S(1)}, f32[4,128,128]{2,1,0:T(8,128)S(1)}, u32[]{:S(2)}, u32[]{:S(2)}) collective-permute-start(f32[4,128,128]{2,1,0:T(8,128)S(1)} %multiply_add_fusion.3), channel_id=1, source_target_pairs={{0,16},{16,32},{32,48},{48,64},{64,80},{80,96},{96,112},{112,128},... | collective-permute-start | bytes 786440 | tf_op jit(solution)/shard_map/while/body/eval_jaxpr/ppermute | solution.py:17
  327.4 38.3 %copy-start.3 = (f32[512]{0:T(512)S(1)}, f32[512]{0:T(512)}, u32[]{:S(2)}) copy-start(f32[512]{0:T(512)} %param.18) | copy-start | bytes 6148
Sparse Core Ops, SparseCore 0:
  11.7 64.7 all-gather.2
  79.7 60.1 all-gather.4
where the time goes:
time: 455 us; the launch traced here: 451 us
  waiting for transfers between devices  247 us (54%)
  matrix products  66.5 us (15%)
  starting transfers between devices  59.6 us (13%)
  blocking collectives  37.5 us (8%)
  other arithmetic  15.5 us (3%)
  between operations  14.2 us (3%)
  local copies, waits for them, and re-layouts  7.01 us (2%)
    ppermute x31, waiting for transfers between devices, shifted(): lax.ppermute(value, axis, [(source, source + steps) for source in range(f...  247 us
    ppermute x31, starting transfers between devices, shifted(): lax.ppermute(value, axis, [(source, source + steps) for source in range(f...  59.5 us
    psum x1, blocking collectives, local(): lax.psum(jnp.sum(mixed * mixed, axis=1), 'head') / (QUERY_HEADS * DH)  37.5 us
    dot_general x25, matrix products, soft_update(): jnp.einsum('kgts,ske->kgte', rounded, value_rows, preferred_element_type=...  35 us
    dot_general x25, matrix products, soft_update(): jnp.einsum('tkgd,skd->kgts', queries, key_rows, preferred_element_type=jn...  29.2 us
  transfers between devices with their start and end apart: 33, of which 31 were waited for; matrix products, arithmetic and copies ran while one was open for 3% of the time, Pallas kernels for 0%

commit v1 on v0

--- a/solution.py
+++ b/solution.py
@@ -9,6 +9,11 @@
 BLOCK = 256
 EPSILON = 1e-06
 NEGATIVE = -1e30
+
+
+def arrange_outputs_for(content):
+    fresh = jax.lax.all_gather(content, "head")
+    return jnp.sum(fresh, axis=0)
 
 
 def shifted(value, axis, steps):
@@ -112,7 +117,7 @@
     entering = lax.fori_loop(0, lax.axis_size("ctx") - 1, advance, jnp.zeros_like(block_state))
     carried = jnp.einsum("thd,hde->the", lifted, entering, precision=lax.Precision.HIGHEST)
     mixed = (local_part + carried).reshape(row_count, width)
-    power = lax.psum(jnp.sum(mixed * mixed, axis=1), "head") / (QUERY_HEADS * DH)
+    power = arrange_outputs_for(jnp.sum(mixed * mixed, axis=1)) / (QUERY_HEADS * DH)
     linear_out = (mixed * lax.rsqrt(power + EPSILON)[:, None] * norm_gain[None, :]).astype(
         jnp.bfloat16
     )

time: 455 us -> 454 us (level)
    psum x1 -> x0, blocking collectives: 37.5 us -> none  [local(): lax.psum(jnp.sum(mixed * mixed, axis=1), 'head') / (QUERY_HEADS * DH)]
    all_gather x0 -> x1, blocking collectives: none -> 36.4 us  [arrange_outputs_for(): fresh = jax.lax.all_gather(content, 'head')]
where the time goes in v1:
time: 454 us; the launch traced here: 450 us
  waiting for transfers between devices  247 us (54%)
  matrix products  66.5 us (15%)
  starting transfers between devices  59.6 us (13%)
  blocking collectives  36.4 us (8%)
  other arithmetic  15.5 us (3%)
  between operations  14.2 us (3%)
  local copies, waits for them, and re-layouts  7.01 us (2%)
    ppermute x31, waiting for transfers between devices, shifted(): lax.ppermute(value, axis, [(source, source + steps) for source in range(f...  247 us
    ppermute x31, starting transfers between devices, shifted(): lax.ppermute(value, axis, [(source, source + steps) for source in range(f...  59.5 us
    all_gather x1, blocking collectives, arrange_outputs_for(): fresh = jax.lax.all_gather(content, 'head')  36.4 us
    dot_general x25, matrix products, soft_update(): jnp.einsum('kgts,ske->kgte', rounded, value_rows, preferred_element_type=...  35 us
    dot_general x25, matrix products, soft_update(): jnp.einsum('tkgd,skd->kgts', queries, key_rows, preferred_element_type=jn...  29.2 us
  transfers between devices with their start and end apart: 33, of which 31 were waited for; matrix products, arithmetic and copies ran while one was open for 3% of the time, Pallas kernels for 0%

profile of v1, /device:TPU:6, one launch (start us, length us, event | category | flops | bytes accessed | tf_op | source)
XLA Modules:
  0.0 450.1 jit_solution(5125077079905695359)
XLA Ops:
  16.4 310.2 %while.9 = (s32[]{:T(128)}, f32[4,128,128]{2,1,0:T(8,128)S(1)}, f32[4]{0:T(128)S(1)}, f32[4,128,128]{2,1,0:T(8,128)S(1)}, s32[]{:T(128)}) while((s32[]{:T(128)}, f32[4,128,128]{2,1,0:T(8,128)S(1)}, f32[4]{0:T(128)S(1)}, f32[4,128,128]{2,1,0:T(8,128)S(1)}, s32[]{:T(128)}) %tuple.86), condition=%wide.region_3.4_spmd, body=%wide.region_2.3_spmd.sunk | while | flops 131074 | bytes 1835125 | solution.py:117
  18.5 7.9 %collective-permute-done = f32[4,128,128]{2,1,0:T(8,128)S(1)} collective-permute-done((f32[4,128,128]{2,1,0:T(8,128)S(1)}, f32[4,128,128]{2,1,0:T(8,128)S(1)}, u32[]{:S(2)}, u32[]{:S(2)}) %collective-permute-start) | collective-permute-done | bytes 262176 | tf_op jit(solution)/shard_map/while/body/eval_jaxpr/ppermute | solution.py:22
  26.4 1.9 collective-permute-start
  28.4 7.9 %collective-permute-done = f32[4,128,128]{2,1,0:T(8,128)S(1)} collective-permute-done((f32[4,128,128]{2,1,0:T(8,128)S(1)}, f32[4,128,128]{2,1,0:T(8,128)S(1)}, u32[]{:S(2)}, u32[]{:S(2)}) %collective-permute-start) | collective-permute-done | bytes 262176 | tf_op jit(solution)/shard_map/while/body/eval_jaxpr/ppermute | solution.py:22
  38.3 8.0 %collective-permute-done = f32[4,128,128]{2,1,0:T(8,128)S(1)} collective-permute-done((f32[4,128,128]{2,1,0:T(8,128)S(1)}, f32[4,128,128]{2,1,0:T(8,128)S(1)}, u32[]{:S(2)}, u32[]{:S(2)}) %collective-permute-start) | collective-permute-done | bytes 262176 | tf_op jit(solution)/shard_map/while/body/eval_jaxpr/ppermute | solution.py:22
  46.4 1.9 collective-permute-start
  48.3 7.9 %collective-permute-done = f32[4,128,128]{2,1,0:T(8,128)S(1)} collective-permute-done((f32[4,128,128]{2,1,0:T(8,128)S(1)}, f32[4,128,128]{2,1,0:T(8,128)S(1)}, u32[]{:S(2)}, u32[]{:S(2)}) %collective-permute-start) | collective-permute-done | bytes 262176 | tf_op jit(solution)/shard_map/while/body/eval_jaxpr/ppermute | solution.py:22
  56.3 1.9 collective-permute-start
  58.2 8.4 %collective-permute-done = f32[4,128,128]{2,1,0:T(8,128)S(1)} collective-permute-done((f32[4,128,128]{2,1,0:T(8,128)S(1)}, f32[4,128,128]{2,1,0:T(8,128)S(1)}, u32[]{:S(2)}, u32[]{:S(2)}) %collective-permute-start) | collective-permute-done | bytes 262176 | tf_op jit(solution)/shard_map/while/body/eval_jaxpr/ppermute | solution.py:22
  68.6 8.7 %collective-permute-done = f32[4,128,128]{2,1,0:T(8,128)S(1)} collective-permute-done((f32[4,128,128]{2,1,0:T(8,128)S(1)}, f32[4,128,128]{2,1,0:T(8,128)S(1)}, u32[]{:S(2)}, u32[]{:S(2)}) %collective-permute-start) | collective-permute-done | bytes 262176 | tf_op jit(solution)/shard_map/while/body/eval_jaxpr/ppermute | solution.py:22
  79.4 7.9 %collective-permute-done = f32[4,128,128]{2,1,0:T(8,128)S(1)} collective-permute-done((f32[4,128,128]{2,1,0:T(8,128)S(1)}, f32[4,128,128]{2,1,0:T(8,128)S(1)}, u32[]{:S(2)}, u32[]{:S(2)}) %collective-permute-start) | collective-permute-done | bytes 262176 | tf_op jit(solution)/shard_map/while/body/eval_jaxpr/ppermute | solution.py:22
  87.4 1.9 collective-permute-start
  89.3 7.9 %collective-permute-done = f32[4,128,128]{2,1,0:T(8,128)S(1)} collective-permute-done((f32[4,128,128]{2,1,0:T(8,128)S(1)}, f32[4,128,128]{2,1,0:T(8,128)S(1)}, u32[]{:S(2)}, u32[]{:S(2)}) %collective-permute-start) | collective-permute-done | bytes 262176 | tf_op jit(solution)/shard_map/while/body/eval_jaxpr/ppermute | solution.py:22
  99.2 8.3 %collective-permute-done = f32[4,128,128]{2,1,0:T(8,128)S(1)} collective-permute-done((f32[4,128,128]{2,1,0:T(8,128)S(1)}, f32[4,128,128]{2,1,0:T(8,128)S(1)}, u32[]{:S(2)}, u32[]{:S(2)}) %collective-permute-start) | collective-permute-done | bytes 262176 | tf_op jit(solution)/shard_map/while/body/eval_jaxpr/ppermute | solution.py:22
  107.6 1.9 collective-permute-start
  109.5 7.9 %collective-permute-done = f32[4,128,128]{2,1,0:T(8,128)S(1)} collective-permute-done((f32[4,128,128]{2,1,0:T(8,128)S(1)}, f32[4,128,128]{2,1,0:T(8,128)S(1)}, u32[]{:S(2)}, u32[]{:S(2)}) %collective-permute-start) | collective-permute-done | bytes 262176 | tf_op jit(solution)/shard_map/while/body/eval_jaxpr/ppermute | solution.py:22
  119.4 7.9 %collective-permute-done = f32[4,128,128]{2,1,0:T(8,128)S(1)} collective-permute-done((f32[4,128,128]{2,1,0:T(8,128)S(1)}, f32[4,128,128]{2,1,0:T(8,128)S(1)}, u32[]{:S(2)}, u32[]{:S(2)}) %collective-permute-start) | collective-permute-done | bytes 262176 | tf_op jit(solution)/shard_map/while/body/eval_jaxpr/ppermute | solution.py:22
  129.3 9.3 %collective-permute-done = f32[4,128,128]{2,1,0:T(8,128)S(1)} collective-permute-done((f32[4,128,128]{2,1,0:T(8,128)S(1)}, f32[4,128,128]{2,1,0:T(8,128)S(1)}, u32[]{:S(2)}, u32[]{:S(2)}) %collective-permute-start) | collective-permute-done | bytes 262176 | tf_op jit(solution)/shard_map/while/body/eval_jaxpr/ppermute | solution.py:22
  140.6 7.9 %collective-permute-done = f32[4,128,128]{2,1,0:T(8,128)S(1)} collective-permute-done((f32[4,128,128]{2,1,0:T(8,128)S(1)}, f32[4,128,128]{2,1,0:T(8,128)S(1)}, u32[]{:S(2)}, u32[]{:S(2)}) %collective-permute-start) | collective-permute-done | bytes 262176 | tf_op jit(solution)/shard_map/while/body/eval_jaxpr/ppermute | solution.py:22
  150.5 7.9 %collective-permute-done = f32[4,128,128]{2,1,0:T(8,128)S(1)} collective-permute-done((f32[4,128,128]{2,1,0:T(8,128)S(1)}, f32[4,128,128]{2,1,0:T(8,128)S(1)}, u32[]{:S(2)}, u32[]{:S(2)}) %collective-permute-start) | collective-permute-done | bytes 262176 | tf_op jit(solution)/shard_map/while/body/eval_jaxpr/ppermute | solution.py:22
  160.4 7.9 %collective-permute-done = f32[4,128,128]{2,1,0:T(8,128)S(1)} collective-permute-done((f32[4,128,128]{2,1,0:T(8,128)S(1)}, f32[4,128,128]{2,1,0:T(8,128)S(1)}, u32[]{:S(2)}, u32[]{:S(2)}) %collective-permute-start) | collective-permute-done | bytes 262176 | tf_op jit(solution)/shard_map/while/body/eval_jaxpr/ppermute | solution.py:22
  170.3 7.9 %collective-permute-done = f32[4,128,128]{2,1,0:T(8,128)S(1)} collective-permute-done((f32[4,128,128]{2,1,0:T(8,128)S(1)}, f32[4,128,128]{2,1,0:T(8,128)S(1)}, u32[]{:S(2)}, u32[]{:S(2)}) %collective-permute-start) | collective-permute-done | bytes 262176 | tf_op jit(solution)/shard_map/while/body/eval_jaxpr/ppermute | solution.py:22
  180.2 7.9 %collective-permute-done = f32[4,128,128]{2,1,0:T(8,128)S(1)} collective-permute-done((f32[4,128,128]{2,1,0:T(8,128)S(1)}, f32[4,128,128]{2,1,0:T(8,128)S(1)}, u32[]{:S(2)}, u32[]{:S(2)}) %collective-permute-start) | collective-permute-done | bytes 262176 | tf_op jit(solution)/shard_map/while/body/eval_jaxpr/ppermute | solution.py:22
  190.1 7.9 %collective-permute-done = f32[4,128,128]{2,1,0:T(8,128)S(1)} collective-permute-done((f32[4,128,128]{2,1,0:T(8,128)S(1)}, f32[4,128,128]{2,1,0:T(8,128)S(1)}, u32[]{:S(2)}, u32[]{:S(2)}) %collective-permute-start) | collective-permute-done | bytes 262176 | tf_op jit(solution)/shard_map/while/body/eval_jaxpr/ppermute | solution.py:22
  200.0 7.9 %collective-permute-done = f32[4,128,128]{2,1,0:T(8,128)S(1)} collective-permute-done((f32[4,128,128]{2,1,0:T(8,128)S(1)}, f32[4,128,128]{2,1,0:T(8,128)S(1)}, u32[]{:S(2)}, u32[]{:S(2)}) %collective-permute-start) | collective-permute-done | bytes 262176 | tf_op jit(solution)/shard_map/while/body/eval_jaxpr/ppermute | solution.py:22
  209.9 7.9 %collective-permute-done = f32[4,128,128]{2,1,0:T(8,128)S(1)} collective-permute-done((f32[4,128,128]{2,1,0:T(8,128)S(1)}, f32[4,128,128]{2,1,0:T(8,128)S(1)}, u32[]{:S(2)}, u32[]{:S(2)}) %collective-permute-start) | collective-permute-done | bytes 262176 | tf_op jit(solution)/shard_map/while/body/eval_jaxpr/ppermute | solution.py:22
  219.8 7.9 %collective-permute-done = f32[4,128,128]{2,1,0:T(8,128)S(1)} collective-permute-done((f32[4,128,128]{2,1,0:T(8,128)S(1)}, f32[4,128,128]{2,1,0:T(8,128)S(1)}, u32[]{:S(2)}, u32[]{:S(2)}) %collective-permute-start) | collective-permute-done | bytes 262176 | tf_op jit(solution)/shard_map/while/body/eval_jaxpr/ppermute | solution.py:22
  229.7 7.9 %collective-permute-done = f32[4,128,128]{2,1,0:T(8,128)S(1)} collective-permute-done((f32[4,128,128]{2,1,0:T(8,128)S(1)}, f32[4,128,128]{2,1,0:T(8,128)S(1)}, u32[]{:S(2)}, u32[]{:S(2)}) %collective-permute-start) | collective-permute-done | bytes 262176 | tf_op jit(solution)/shard_map/while/body/eval_jaxpr/ppermute | solution.py:22
  239.6 7.9 %collective-permute-done = f32[4,128,128]{2,1,0:T(8,128)S(1)} collective-permute-done((f32[4,128,128]{2,1,0:T(8,128)S(1)}, f32[4,128,128]{2,1,0:T(8,128)S(1)}, u32[]{:S(2)}, u32[]{:S(2)}) %collective-permute-start) | collective-permute-done | bytes 262176 | tf_op jit(solution)/shard_map/while/body/eval_jaxpr/ppermute | solution.py:22
  249.5 7.9 %collective-permute-done = f32[4,128,128]{2,1,0:T(8,128)S(1)} collective-permute-done((f32[4,128,128]{2,1,0:T(8,128)S(1)}, f32[4,128,128]{2,1,0:T(8,128)S(1)}, u32[]{:S(2)}, u32[]{:S(2)}) %collective-permute-start) | collective-permute-done | bytes 262176 | tf_op jit(solution)/shard_map/while/body/eval_jaxpr/ppermute | solution.py:22
  259.4 7.9 %collective-permute-done = f32[4,128,128]{2,1,0:T(8,128)S(1)} collective-permute-done((f32[4,128,128]{2,1,0:T(8,128)S(1)}, f32[4,128,128]{2,1,0:T(8,128)S(1)}, u32[]{:S(2)}, u32[]{:S(2)}) %collective-permute-start) | collective-permute-done | bytes 262176 | tf_op jit(solution)/shard_map/while/body/eval_jaxpr/ppermute | solution.py:22
  269.3 7.9 %collective-permute-done = f32[4,128,128]{2,1,0:T(8,128)S(1)} collective-permute-done((f32[4,128,128]{2,1,0:T(8,128)S(1)}, f32[4,128,128]{2,1,0:T(8,128)S(1)}, u32[]{:S(2)}, u32[]{:S(2)}) %collective-permute-start) | collective-permute-done | bytes 262176 | tf_op jit(solution)/shard_map/while/body/eval_jaxpr/ppermute | solution.py:22
  279.2 7.9 %collective-permute-done = f32[4,128,128]{2,1,0:T(8,128)S(1)} collective-permute-done((f32[4,128,128]{2,1,0:T(8,128)S(1)}, f32[4,128,128]{2,1,0:T(8,128)S(1)}, u32[]{:S(2)}, u32[]{:S(2)}) %collective-permute-start) | collective-permute-done | bytes 262176 | tf_op jit(solution)/shard_map/while/body/eval_jaxpr/ppermute | solution.py:22
  289.1 7.9 %collective-permute-done = f32[4,128,128]{2,1,0:T(8,128)S(1)} collective-permute-done((f32[4,128,128]{2,1,0:T(8,128)S(1)}, f32[4,128,128]{2,1,0:T(8,128)S(1)}, u32[]{:S(2)}, u32[]{:S(2)}) %collective-permute-start) | collective-permute-done | bytes 262176 | tf_op jit(solution)/shard_map/while/body/eval_jaxpr/ppermute | solution.py:22
  299.0 7.9 %collective-permute-done = f32[4,128,128]{2,1,0:T(8,128)S(1)} collective-permute-done((f32[4,128,128]{2,1,0:T(8,128)S(1)}, f32[4,128,128]{2,1,0:T(8,128)S(1)}, u32[]{:S(2)}, u32[]{:S(2)}) %collective-permute-start) | collective-permute-done | bytes 262176 | tf_op jit(solution)/shard_map/while/body/eval_jaxpr/ppermute | solution.py:22
  308.9 7.9 %collective-permute-done = f32[4,128,128]{2,1,0:T(8,128)S(1)} collective-permute-done((f32[4,128,128]{2,1,0:T(8,128)S(1)}, f32[4,128,128]{2,1,0:T(8,128)S(1)}, u32[]{:S(2)}, u32[]{:S(2)}) %collective-permute-start) | collective-permute-done | bytes 262176 | tf_op jit(solution)/shard_map/while/body/eval_jaxpr/ppermute | solution.py:22
  318.8 7.9 %collective-permute-done = f32[4,128,128]{2,1,0:T(8,128)S(1)} collective-permute-done((f32[4,128,128]{2,1,0:T(8,128)S(1)}, f32[4,128,128]{2,1,0:T(8,128)S(1)}, u32[]{:S(2)}, u32[]{:S(2)}) %collective-permute-start) | collective-permute-done | bytes 262176 | tf_op jit(solution)/shard_map/while/body/eval_jaxpr/ppermute | solution.py:22
  328.2 36.4 %all-gather.1 = f32[16,1,256]{2,1,0:T(1,128)S(1)} all-gather(f32[1,1,256]{2,1,0:T(1,128)S(1)} %bitcast.124), channel_id=2, replica_groups=mesh['ctx'=32,'head'=16] {'head'}, dimensions={0}, use_global_device_ids=true | all-gather | bytes 17408 | tf_op jit(solution)/shard_map/all_gather | solution.py:15
  365.6 76.8 %while.36 = (s32[]{:T(128)}, f32[4,256]{1,0:T(4,128)S(1)}, f32[4,256]{1,0:T(4,128)S(1)}, f32[4,256,128]{2,1,0:T(8,128)S(1)}, s32[]{:T(128)}, /*index=5*/bf16[819...) while((s32[]{:T(128)}, f32[4,256]{1,0:T(4,128)S(1)}, ...), condition=%wide.region_11.12_spmd.clone, body=%wide.region_6.11_spmd.clone.sunk | while | flops 137431552 | bytes 4922689 | solution.py:79
  365.6 3.0 conditional.3
  368.7 3.0 conditional.3
  371.7 3.0 conditional.3
  374.8 3.0 conditional.3
  377.8 3.0 conditional.3
  380.9 3.0 conditional.3
  383.9 3.0 conditional.3
  387.0 3.0 conditional.3
  390.0 3.0 conditional.3
  393.1 3.0 conditional.3
  396.2 3.0 conditional.3
  399.2 3.0 conditional.3
  402.3 3.0 conditional.3
  405.3 3.0 conditional.3
  408.4 3.0 conditional.3
  411.4 3.0 conditional.3
  414.5 3.0 conditional.3
  417.6 3.0 conditional.3
  420.6 3.0 conditional.3
  423.7 3.0 conditional.3
  426.7 3.0 conditional.3
  429.8 3.0 conditional.3
  432.8 3.0 conditional.3
  435.9 3.0 conditional.3
  439.0 3.0 conditional.3
  (341 shorter events, 139.1 us)
Async XLA Ops:
  7.2 1.0 copy-start
  7.2 8.2 %copy-start.1 = (bf16[256,512]{1,0:T(8,128)(2,1)S(1)}, bf16[256,512]{1,0:T(8,128)(2,1)}, u32[]{:S(2)}) copy-start(bf16[256,512]{1,0:T(8,128)(2,1)} %param.14) | copy-start | bytes 786436
  7.2 9.0 %copy-start.2 = (bf16[256,512]{1,0:T(8,128)(2,1)S(1)}, bf16[256,512]{1,0:T(8,128)(2,1)}, u32[]{:S(2)}) copy-start(bf16[256,512]{1,0:T(8,128)(2,1)} %param.16) | copy-start | bytes 786436
  7.2 358.3 %all-gather.5.cloned.1.call-start = ((), (), s32[]{:S(2)}) async-start(), calls=%async_computation | async-start | bytes 2162688 | tf_op jit(solution)/shard_map/all_gather | solution.py:161
  8.9 356.6 %all-gather.7.cloned.1.call-start = ((), (), s32[]{:S(2)}) async-start(), calls=%async_computation.1 | async-start | bytes 2162688 | tf_op jit(solution)/shard_map/all_gather | solution.py:162
  16.5 9.8 %collective-permute-start = (f32[4,128,128]{2,1,0:T(8,128)S(1)}, f32[4,128,128]{2,1,0:T(8,128)S(1)}, u32[]{:S(2)}, u32[]{:S(2)}) collective-permute-start(f32[4,128,128]{2,1,0:T(8,128)S(1)} %multiply_add_fusion.3), channel_id=1, source_target_pairs={{0,16},{16,32},{32,48},{48,64},{64,80},{80,96},{96,112},{112,128},... | collective-permute-start | bytes 786440 | tf_op jit(solution)/shard_map/while/body/eval_jaxpr/ppermute | solution.py:22
  26.4 9.8 %collective-permute-start = (f32[4,128,128]{2,1,0:T(8,128)S(1)}, f32[4,128,128]{2,1,0:T(8,128)S(1)}, u32[]{:S(2)}, u32[]{:S(2)}) collective-permute-start(f32[4,128,128]{2,1,0:T(8,128)S(1)} %multiply_add_fusion.3), channel_id=1, source_target_pairs={{0,16},{16,32},{32,48},{48,64},{64,80},{80,96},{96,112},{112,128},... | collective-permute-start | bytes 786440 | tf_op jit(solution)/shard_map/while/body/eval_jaxpr/ppermute | solution.py:22
  36.3 10.0 %collective-permute-start = (f32[4,128,128]{2,1,0:T(8,128)S(1)}, f32[4,128,128]{2,1,0:T(8,128)S(1)}, u32[]{:S(2)}, u32[]{:S(2)}) collective-permute-start(f32[4,128,128]{2,1,0:T(8,128)S(1)} %multiply_add_fusion.3), channel_id=1, source_target_pairs={{0,16},{16,32},{32,48},{48,64},{64,80},{80,96},{96,112},{112,128},... | collective-permute-start | bytes 786440 | tf_op jit(solution)/shard_map/while/body/eval_jaxpr/ppermute | solution.py:22
  46.4 9.8 %collective-permute-start = (f32[4,128,128]{2,1,0:T(8,128)S(1)}, f32[4,128,128]{2,1,0:T(8,128)S(1)}, u32[]{:S(2)}, u32[]{:S(2)}) collective-permute-start(f32[4,128,128]{2,1,0:T(8,128)S(1)} %multiply_add_fusion.3), channel_id=1, source_target_pairs={{0,16},{16,32},{32,48},{48,64},{64,80},{80,96},{96,112},{112,128},... | collective-permute-start | bytes 786440 | tf_op jit(solution)/shard_map/while/body/eval_jaxpr/ppermute | solution.py:22
  56.3 10.3 %collective-permute-start = (f32[4,128,128]{2,1,0:T(8,128)S(1)}, f32[4,128,128]{2,1,0:T(8,128)S(1)}, u32[]{:S(2)}, u32[]{:S(2)}) collective-permute-start(f32[4,128,128]{2,1,0:T(8,128)S(1)} %multiply_add_fusion.3), channel_id=1, source_target_pairs={{0,16},{16,32},{32,48},{48,64},{64,80},{80,96},{96,112},{112,128},... | collective-permute-start | bytes 786440 | tf_op jit(solution)/shard_map/while/body/eval_jaxpr/ppermute | solution.py:22
  66.7 10.7 %collective-permute-start = (f32[4,128,128]{2,1,0:T(8,128)S(1)}, f32[4,128,128]{2,1,0:T(8,128)S(1)}, u32[]{:S(2)}, u32[]{:S(2)}) collective-permute-start(f32[4,128,128]{2,1,0:T(8,128)S(1)} %multiply_add_fusion.3), channel_id=1, source_target_pairs={{0,16},{16,32},{32,48},{48,64},{64,80},{80,96},{96,112},{112,128},... | collective-permute-start | bytes 786440 | tf_op jit(solution)/shard_map/while/body/eval_jaxpr/ppermute | solution.py:22
  77.5 9.8 %collective-permute-start = (f32[4,128,128]{2,1,0:T(8,128)S(1)}, f32[4,128,128]{2,1,0:T(8,128)S(1)}, u32[]{:S(2)}, u32[]{:S(2)}) collective-permute-start(f32[4,128,128]{2,1,0:T(8,128)S(1)} %multiply_add_fusion.3), channel_id=1, source_target_pairs={{0,16},{16,32},{32,48},{48,64},{64,80},{80,96},{96,112},{112,128},... | collective-permute-start | bytes 786440 | tf_op jit(solution)/shard_map/while/body/eval_jaxpr/ppermute | solution.py:22
  87.4 9.8 %collective-permute-start = (f32[4,128,128]{2,1,0:T(8,128)S(1)}, f32[4,128,128]{2,1,0:T(8,128)S(1)}, u32[]{:S(2)}, u32[]{:S(2)}) collective-permute-start(f32[4,128,128]{2,1,0:T(8,128)S(1)} %multiply_add_fusion.3), channel_id=1, source_target_pairs={{0,16},{16,32},{32,48},{48,64},{64,80},{80,96},{96,112},{112,128},... | collective-permute-start | bytes 786440 | tf_op jit(solution)/shard_map/while/body/eval_jaxpr/ppermute | solution.py:22
  97.3 10.2 %collective-permute-start = (f32[4,128,128]{2,1,0:T(8,128)S(1)}, f32[4,128,128]{2,1,0:T(8,128)S(1)}, u32[]{:S(2)}, u32[]{:S(2)}) collective-permute-start(f32[4,128,128]{2,1,0:T(8,128)S(1)} %multiply_add_fusion.3), channel_id=1, source_target_pairs={{0,16},{16,32},{32,48},{48,64},{64,80},{80,96},{96,112},{112,128},... | collective-permute-start | bytes 786440 | tf_op jit(solution)/shard_map/while/body/eval_jaxpr/ppermute | solution.py:22
  107.6 9.8 %collective-permute-start = (f32[4,128,128]{2,1,0:T(8,128)S(1)}, f32[4,128,128]{2,1,0:T(8,128)S(1)}, u32[]{:S(2)}, u32[]{:S(2)}) collective-permute-start(f32[4,128,128]{2,1,0:T(8,128)S(1)} %multiply_add_fusion.3), channel_id=1, source_target_pairs={{0,16},{16,32},{32,48},{48,64},{64,80},{80,96},{96,112},{112,128},... | collective-permute-start | bytes 786440 | tf_op jit(solution)/shard_map/while/body/eval_jaxpr/ppermute | solution.py:22
  117.5 9.8 %collective-permute-start = (f32[4,128,128]{2,1,0:T(8,128)S(1)}, f32[4,128,128]{2,1,0:T(8,128)S(1)}, u32[]{:S(2)}, u32[]{:S(2)}) collective-permute-start(f32[4,128,128]{2,1,0:T(8,128)S(1)} %multiply_add_fusion.3), channel_id=1, source_target_pairs={{0,16},{16,32},{32,48},{48,64},{64,80},{80,96},{96,112},{112,128},... | collective-permute-start | bytes 786440 | tf_op jit(solution)/shard_map/while/body/eval_jaxpr/ppermute | solution.py:22
  127.4 11.2 %collective-permute-start = (f32[4,128,128]{2,1,0:T(8,128)S(1)}, f32[4,128,128]{2,1,0:T(8,128)S(1)}, u32[]{:S(2)}, u32[]{:S(2)}) collective-permute-start(f32[4,128,128]{2,1,0:T(8,128)S(1)} %multiply_add_fusion.3), channel_id=1, source_target_pairs={{0,16},{16,32},{32,48},{48,64},{64,80},{80,96},{96,112},{112,128},... | collective-permute-start | bytes 786440 | tf_op jit(solution)/shard_map/while/body/eval_jaxpr/ppermute | solution.py:22
  138.7 9.8 %collective-permute-start = (f32[4,128,128]{2,1,0:T(8,128)S(1)}, f32[4,128,128]{2,1,0:T(8,128)S(1)}, u32[]{:S(2)}, u32[]{:S(2)}) collective-permute-start(f32[4,128,128]{2,1,0:T(8,128)S(1)} %multiply_add_fusion.3), channel_id=1, source_target_pairs={{0,16},{16,32},{32,48},{48,64},{64,80},{80,96},{96,112},{112,128},... | collective-permute-start | bytes 786440 | tf_op jit(solution)/shard_map/while/body/eval_jaxpr/ppermute | solution.py:22
  148.6 9.8 %collective-permute-start = (f32[4,128,128]{2,1,0:T(8,128)S(1)}, f32[4,128,128]{2,1,0:T(8,128)S(1)}, u32[]{:S(2)}, u32[]{:S(2)}) collective-permute-start(f32[4,128,128]{2,1,0:T(8,128)S(1)} %multiply_add_fusion.3), channel_id=1, source_target_pairs={{0,16},{16,32},{32,48},{48,64},{64,80},{80,96},{96,112},{112,128},... | collective-permute-start | bytes 786440 | tf_op jit(solution)/shard_map/while/body/eval_jaxpr/ppermute | solution.py:22
  158.5 9.8 %collective-permute-start = (f32[4,128,128]{2,1,0:T(8,128)S(1)}, f32[4,128,128]{2,1,0:T(8,128)S(1)}, u32[]{:S(2)}, u32[]{:S(2)}) collective-permute-start(f32[4,128,128]{2,1,0:T(8,128)S(1)} %multiply_add_fusion.3), channel_id=1, source_target_pairs={{0,16},{16,32},{32,48},{48,64},{64,80},{80,96},{96,112},{112,128},... | collective-permute-start | bytes 786440 | tf_op jit(solution)/shard_map/while/body/eval_jaxpr/ppermute | solution.py:22
  168.4 9.8 %collective-permute-start = (f32[4,128,128]{2,1,0:T(8,128)S(1)}, f32[4,128,128]{2,1,0:T(8,128)S(1)}, u32[]{:S(2)}, u32[]{:S(2)}) collective-permute-start(f32[4,128,128]{2,1,0:T(8,128)S(1)} %multiply_add_fusion.3), channel_id=1, source_target_pairs={{0,16},{16,32},{32,48},{48,64},{64,80},{80,96},{96,112},{112,128},... | collective-permute-start | bytes 786440 | tf_op jit(solution)/shard_map/while/body/eval_jaxpr/ppermute | solution.py:22
  178.3 9.8 %collective-permute-start = (f32[4,128,128]{2,1,0:T(8,128)S(1)}, f32[4,128,128]{2,1,0:T(8,128)S(1)}, u32[]{:S(2)}, u32[]{:S(2)}) collective-permute-start(f32[4,128,128]{2,1,0:T(8,128)S(1)} %multiply_add_fusion.3), channel_id=1, source_target_pairs={{0,16},{16,32},{32,48},{48,64},{64,80},{80,96},{96,112},{112,128},... | collective-permute-start | bytes 786440 | tf_op jit(solution)/shard_map/while/body/eval_jaxpr/ppermute | solution.py:22
  188.2 9.8 %collective-permute-start = (f32[4,128,128]{2,1,0:T(8,128)S(1)}, f32[4,128,128]{2,1,0:T(8,128)S(1)}, u32[]{:S(2)}, u32[]{:S(2)}) collective-permute-start(f32[4,128,128]{2,1,0:T(8,128)S(1)} %multiply_add_fusion.3), channel_id=1, source_target_pairs={{0,16},{16,32},{32,48},{48,64},{64,80},{80,96},{96,112},{112,128},... | collective-permute-start | bytes 786440 | tf_op jit(solution)/shard_map/while/body/eval_jaxpr/ppermute | solution.py:22
  198.1 9.8 %collective-permute-start = (f32[4,128,128]{2,1,0:T(8,128)S(1)}, f32[4,128,128]{2,1,0:T(8,128)S(1)}, u32[]{:S(2)}, u32[]{:S(2)}) collective-permute-start(f32[4,128,128]{2,1,0:T(8,128)S(1)} %multiply_add_fusion.3), channel_id=1, source_target_pairs={{0,16},{16,32},{32,48},{48,64},{64,80},{80,96},{96,112},{112,128},... | collective-permute-start | bytes 786440 | tf_op jit(solution)/shard_map/while/body/eval_jaxpr/ppermute | solution.py:22
  208.0 9.8 %collective-permute-start = (f32[4,128,128]{2,1,0:T(8,128)S(1)}, f32[4,128,128]{2,1,0:T(8,128)S(1)}, u32[]{:S(2)}, u32[]{:S(2)}) collective-permute-start(f32[4,128,128]{2,1,0:T(8,128)S(1)} %multiply_add_fusion.3), channel_id=1, source_target_pairs={{0,16},{16,32},{32,48},{48,64},{64,80},{80,96},{96,112},{112,128},... | collective-permute-start | bytes 786440 | tf_op jit(solution)/shard_map/while/body/eval_jaxpr/ppermute | solution.py:22
  217.9 9.8 %collective-permute-start = (f32[4,128,128]{2,1,0:T(8,128)S(1)}, f32[4,128,128]{2,1,0:T(8,128)S(1)}, u32[]{:S(2)}, u32[]{:S(2)}) collective-permute-start(f32[4,128,128]{2,1,0:T(8,128)S(1)} %multiply_add_fusion.3), channel_id=1, source_target_pairs={{0,16},{16,32},{32,48},{48,64},{64,80},{80,96},{96,112},{112,128},... | collective-permute-start | bytes 786440 | tf_op jit(solution)/shard_map/while/body/eval_jaxpr/ppermute | solution.py:22
  227.8 9.8 %collective-permute-start = (f32[4,128,128]{2,1,0:T(8,128)S(1)}, f32[4,128,128]{2,1,0:T(8,128)S(1)}, u32[]{:S(2)}, u32[]{:S(2)}) collective-permute-start(f32[4,128,128]{2,1,0:T(8,128)S(1)} %multiply_add_fusion.3), channel_id=1, source_target_pairs={{0,16},{16,32},{32,48},{48,64},{64,80},{80,96},{96,112},{112,128},... | collective-permute-start | bytes 786440 | tf_op jit(solution)/shard_map/while/body/eval_jaxpr/ppermute | solution.py:22
  237.7 9.8 %collective-permute-start = (f32[4,128,128]{2,1,0:T(8,128)S(1)}, f32[4,128,128]{2,1,0:T(8,128)S(1)}, u32[]{:S(2)}, u32[]{:S(2)}) collective-permute-start(f32[4,128,128]{2,1,0:T(8,128)S(1)} %multiply_add_fusion.3), channel_id=1, source_target_pairs={{0,16},{16,32},{32,48},{48,64},{64,80},{80,96},{96,112},{112,128},... | collective-permute-start | bytes 786440 | tf_op jit(solution)/shard_map/while/body/eval_jaxpr/ppermute | solution.py:22
  247.5 9.8 %collective-permute-start = (f32[4,128,128]{2,1,0:T(8,128)S(1)}, f32[4,128,128]{2,1,0:T(8,128)S(1)}, u32[]{:S(2)}, u32[]{:S(2)}) collective-permute-start(f32[4,128,128]{2,1,0:T(8,128)S(1)} %multiply_add_fusion.3), channel_id=1, source_target_pairs={{0,16},{16,32},{32,48},{48,64},{64,80},{80,96},{96,112},{112,128},... | collective-permute-start | bytes 786440 | tf_op jit(solution)/shard_map/while/body/eval_jaxpr/ppermute | solution.py:22
  257.4 9.8 %collective-permute-start = (f32[4,128,128]{2,1,0:T(8,128)S(1)}, f32[4,128,128]{2,1,0:T(8,128)S(1)}, u32[]{:S(2)}, u32[]{:S(2)}) collective-permute-start(f32[4,128,128]{2,1,0:T(8,128)S(1)} %multiply_add_fusion.3), channel_id=1, source_target_pairs={{0,16},{16,32},{32,48},{48,64},{64,80},{80,96},{96,112},{112,128},... | collective-permute-start | bytes 786440 | tf_op jit(solution)/shard_map/while/body/eval_jaxpr/ppermute | solution.py:22
  267.3 9.8 %collective-permute-start = (f32[4,128,128]{2,1,0:T(8,128)S(1)}, f32[4,128,128]{2,1,0:T(8,128)S(1)}, u32[]{:S(2)}, u32[]{:S(2)}) collective-permute-start(f32[4,128,128]{2,1,0:T(8,128)S(1)} %multiply_add_fusion.3), channel_id=1, source_target_pairs={{0,16},{16,32},{32,48},{48,64},{64,80},{80,96},{96,112},{112,128},... | collective-permute-start | bytes 786440 | tf_op jit(solution)/shard_map/while/body/eval_jaxpr/ppermute | solution.py:22
  277.2 9.8 %collective-permute-start = (f32[4,128,128]{2,1,0:T(8,128)S(1)}, f32[4,128,128]{2,1,0:T(8,128)S(1)}, u32[]{:S(2)}, u32[]{:S(2)}) collective-permute-start(f32[4,128,128]{2,1,0:T(8,128)S(1)} %multiply_add_fusion.3), channel_id=1, source_target_pairs={{0,16},{16,32},{32,48},{48,64},{64,80},{80,96},{96,112},{112,128},... | collective-permute-start | bytes 786440 | tf_op jit(solution)/shard_map/while/body/eval_jaxpr/ppermute | solution.py:22
  287.1 9.8 %collective-permute-start = (f32[4,128,128]{2,1,0:T(8,128)S(1)}, f32[4,128,128]{2,1,0:T(8,128)S(1)}, u32[]{:S(2)}, u32[]{:S(2)}) collective-permute-start(f32[4,128,128]{2,1,0:T(8,128)S(1)} %multiply_add_fusion.3), channel_id=1, source_target_pairs={{0,16},{16,32},{32,48},{48,64},{64,80},{80,96},{96,112},{112,128},... | collective-permute-start | bytes 786440 | tf_op jit(solution)/shard_map/while/body/eval_jaxpr/ppermute | solution.py:22
  297.0 9.8 %collective-permute-start = (f32[4,128,128]{2,1,0:T(8,128)S(1)}, f32[4,128,128]{2,1,0:T(8,128)S(1)}, u32[]{:S(2)}, u32[]{:S(2)}) collective-permute-start(f32[4,128,128]{2,1,0:T(8,128)S(1)} %multiply_add_fusion.3), channel_id=1, source_target_pairs={{0,16},{16,32},{32,48},{48,64},{64,80},{80,96},{96,112},{112,128},... | collective-permute-start | bytes 786440 | tf_op jit(solution)/shard_map/while/body/eval_jaxpr/ppermute | solution.py:22
  306.9 9.8 %collective-permute-start = (f32[4,128,128]{2,1,0:T(8,128)S(1)}, f32[4,128,128]{2,1,0:T(8,128)S(1)}, u32[]{:S(2)}, u32[]{:S(2)}) collective-permute-start(f32[4,128,128]{2,1,0:T(8,128)S(1)} %multiply_add_fusion.3), channel_id=1, source_target_pairs={{0,16},{16,32},{32,48},{48,64},{64,80},{80,96},{96,112},{112,128},... | collective-permute-start | bytes 786440 | tf_op jit(solution)/shard_map/while/body/eval_jaxpr/ppermute | solution.py:22
  316.8 9.8 %collective-permute-start = (f32[4,128,128]{2,1,0:T(8,128)S(1)}, f32[4,128,128]{2,1,0:T(8,128)S(1)}, u32[]{:S(2)}, u32[]{:S(2)}) collective-permute-start(f32[4,128,128]{2,1,0:T(8,128)S(1)} %multiply_add_fusion.3), channel_id=1, source_target_pairs={{0,16},{16,32},{32,48},{48,64},{64,80},{80,96},{96,112},{112,128},... | collective-permute-start | bytes 786440 | tf_op jit(solution)/shard_map/while/body/eval_jaxpr/ppermute | solution.py:22
  327.4 37.3 %copy-start.3 = (f32[512]{0:T(512)S(1)}, f32[512]{0:T(512)}, u32[]{:S(2)}) copy-start(f32[512]{0:T(512)} %param.18) | copy-start | bytes 6148
Sparse Core Ops, SparseCore 0:
  11.7 64.7 all-gather.4
  79.7 60.1 all-gather.6
